TPU v7x, 32 devices: a whole 2x2x4 slice. The times are simulated.
32 devices in a mesh: tm: 4 (over y, x), chan: 8 (over z, core).
Axes of the slice: x: 2, y: 2, z: 4, core: 2. Of those that a mesh axis runs over, the one named last changes fastest.
Arguments:
- strain: bfloat16 [256, 16384], P('chan', 'tm'), may hold values from -6 to 6
- fir_taps: bfloat16 [256, 256], P('chan'), may hold values from -0.375 to 0.375
Outputs:
- stacked: float32 [2, 256, 256, 256], P(None, 'tm', 'chan')
All inputs are finite; a program needn't handle non-finite values.
Results may differ from a plain program's by a relative error of at most 0.0062.
Values may be sent and summed in bfloat16 or wider, within the bound.
No kernel may reach another device: no remote copies, remote signals or barrier semaphores. Data moves between devices by JAX's collectives and lax.ppermute only.
A program may use at most 128 MiB of HBM per device.

v0:
```python
import math
import jax
import jax.numpy as jnp
from jax import lax
from jax.sharding import PartitionSpec as P

SEG = 512


def shifted(value, axis, by):
    size = lax.axis_size(axis)
    pairs = [(i, i + by) for i in range(size) if 0 <= i + by < size]
    return lax.ppermute(value, axis, pairs)


def make_table():
    sample_idx = jnp.arange(SEG, dtype=jnp.int32)
    bin_idx = jnp.arange(SEG // 2, dtype=jnp.int32)
    phases = sample_idx[:, None] * bin_idx[None, :] % SEG
    angles = phases.astype(jnp.float32) * (2.0 * math.pi / SEG)
    window = 0.5 - 0.5 * jnp.cos(sample_idx.astype(jnp.float32) * (2.0 * math.pi / SEG))
    cosine = window[:, None] * jnp.cos(angles)
    sine_part = -window[:, None] * jnp.sin(angles)
    return jnp.stack([cosine, sine_part], axis=1).astype(jnp.bfloat16)


def toeplitz(fir_taps):
    tap_count = fir_taps.shape[1]
    row_idx = jnp.arange(2 * tap_count, dtype=jnp.int32)[:, None]
    col_idx = jnp.arange(tap_count, dtype=jnp.int32)[None, :]
    lag_idx = col_idx + tap_count - row_idx
    valid = (lag_idx >= 0) & (lag_idx < tap_count)
    picked = jnp.take(fir_taps, jnp.clip(lag_idx, 0, tap_count - 1), axis=1)
    return jnp.where(valid[None, :, :], picked, jnp.zeros_like(picked))


def cross_block(own_bins, other_bins):
    swapped = jnp.stack([-other_bins[:, 1], other_bins[:, 0]], axis=1)
    real_part = jnp.einsum(
        "kpsi,kpsj->kij", own_bins, other_bins, preferred_element_type=jnp.float32
    )
    imag_part = jnp.einsum("kpsi,kpsj->kij", own_bins, swapped, preferred_element_type=jnp.float32)
    return jnp.stack([real_part, imag_part], axis=0)


def shards(strain, fir_taps):
    tap_count = fir_taps.shape[1]
    channels = strain.shape[0]
    previous = shifted(strain[:, -tap_count:], "tm", 1)
    extended = jnp.concatenate([previous, strain], axis=1)
    blocks = extended.reshape(channels, -1, tap_count)
    block_pairs = jnp.concatenate([blocks[:, :-1], blocks[:, 1:]], axis=2)
    filtered = jnp.einsum(
        "cbr,cri->cbi", block_pairs, toeplitz(fir_taps), preferred_element_type=jnp.float32
    )
    whitened = filtered.reshape(channels, -1).astype(jnp.bfloat16)
    segments = whitened.reshape(channels, whitened.shape[1] // SEG, SEG)
    spectra = jnp.einsum(
        "csn,npk->kpsc", segments, make_table(), preferred_element_type=jnp.float32
    ).astype(jnp.bfloat16)
    gathered = lax.all_gather(spectra, "chan", axis=3, tiled=True)
    all_bins = lax.all_to_all(gathered, "tm", split_axis=0, concat_axis=2, tiled=True)
    factor = 1.0 / (all_bins.shape[2] * SEG)
    first_col = lax.axis_index("chan") * channels
    own_bins = lax.dynamic_slice_in_dim(all_bins, first_col, channels, 3)
    result = cross_block(own_bins, all_bins) * factor
    return result


def solution(mesh):
    placed = (P("chan", "tm"), P("chan", None))
    return jax.shard_map(
        shards, mesh=mesh, in_specs=placed, out_specs=P(None, "tm", "chan", None), check_vma=False
    )
```

profile of v0, /device:TPU:0, one launch (start us, length us, event | category | flops | bytes accessed | tf_op | source)
XLA Modules:
  0.0 581.4 jit_solution(17817019750190096485)
XLA Ops:
  6.5 0.0 copy-start.1
  6.5 0.0 all-gather.2.cloned.1.call-start
  6.5 0.7 slice.15
  7.3 4.8 collective-permute-start
  12.2 0.1 fusion.24
  12.4 0.3 copy.28
  12.7 0.1 broadcast_clamp_fusion
  12.7 2.3 multiply_convert_fusion
  15.0 0.4 fusion.37
  15.4 0.0 copy-done.1
  15.4 0.1 copy.16
  15.5 454.0 %gather_fusion = bf16[131072,32]{1,0:T(8,128)(2,1)} fusion(bf16[32,256]{0,1:T(8,128)(2,1)S(1)} %copy.16, s32[131072]{0:T(1024)S(1)} %broadcast_clamp_fusion), kind=kCustom, calls=%fused_computation | custom fusion | bytes 17301504 | tf_op jit(solution)/shard_map/jit(_take)/gather | solution.py:33
  469.5 0.0 copy-start
  469.5 30.7 %copy.17 = bf16[512,256,32]{1,0,2:T(8,128)(2,1)} copy(bf16[512,256,32]{2,1,0:T(8,128)(2,1)} %bitcast.35) | data formatting | bytes 16777216 | tf_op jit(solution)/shard_map/jit(_take)/gather | solution.py:33
  500.2 0.0 collective-permute-done
  500.3 0.0 copy-done
  500.3 0.1 reshape.212
  500.4 0.1 fusion.49
  500.6 4.7 fusion.15
  505.3 0.1 convert_element_type.45
  505.4 1.0 fusion.18
  506.4 0.0 all-gather.2.cloned.1.call-update
  506.4 29.6 %all-gather.2.cloned.1.call-done = bf16[256,2,8,256]{0,3,2,1:T(8,128)(2,1)} async-done(((bf16[256,2,8,32]{0,3,2,1:T(8,128)(2,1)}), bf16[256,2,8,256]{0,3,2,1:T(8,128)(2,1)}) %all-gather.2.cloned.1.call-update) | async-done | bytes 2097168 | tf_op jit(solution)/shard_map/all_gather | solution.py:61
  536.0 4.5 copy.19
  540.5 3.6 all-to-all-start
  544.1 25.5 %all-to-all-done = bf16[256,2,8,256]{3,2,1,0:T(8,128)(2,1)S(1)} async-done(((bf16[256,2,8,256]{3,2,1,0:T(8,128)(2,1)}), bf16[256,2,8,256]{3,2,1,0:T(8,128)(2,1)S(1)}, u32[]{:S(2)}, u32[]{:S(2)}) %all-to-all-start) | async-done | bytes 2097184 | tf_op jit(solution)/shard_map/all_to_all | solution.py:62
  569.6 0.3 copy.34
  569.9 0.1 slice_negate_fusion
  570.0 1.0 convolution_bitcast_fusion
  571.1 1.0 fusion.12
  572.1 2.5 maximum_multiply_fusion
  (4 shorter events, 0.1 us)
Async XLA Ops:
  6.5 8.9 %copy-start.1 = (bf16[32,256]{1,0:T(8,128)(2,1)S(1)}, bf16[32,256]{1,0:T(8,128)(2,1)}, u32[]{:S(2)}) copy-start(bf16[32,256]{1,0:T(8,128)(2,1)} %param.3) | copy-start | bytes 49156
  6.5 529.5 %all-gather.2.cloned.1.call-start = ((), (), s32[]{:S(2)}) async-start(), calls=%async_computation.1 | async-start | bytes 2359296 | tf_op jit(solution)/shard_map/all_gather | solution.py:61
  7.3 493.0 %collective-permute-start = (bf16[32,256]{1,0:T(8,128)(2,1)S(1)}, bf16[32,256]{1,0:T(8,128)(2,1)S(1)}, u32[]{:S(2)}, u32[]{:S(2)}) collective-permute-start(bf16[32,256]{1,0:T(8,128)(2,1)S(1)} %slice.15), channel_id=1, source_target_pairs={{0,8},{8,16},{16,24},{1,9},{9,17},{17,25},{2,10},{10,18},{18,26},{... | collective-permute-start | bytes 49160 | tf_op jit(solution)/shard_map/ppermute | solution.py:13
  469.5 30.7 %copy-start = (bf16[32,4096]{1,0:T(8,128)(2,1)S(1)}, bf16[32,4096]{1,0:T(8,128)(2,1)}, u32[]{:S(2)}) copy-start(bf16[32,4096]{1,0:T(8,128)(2,1)} %param.2) | copy-start | bytes 786436
  540.5 29.1 %all-to-all-start = ((bf16[256,2,8,256]{3,2,1,0:T(8,128)(2,1)}), bf16[256,2,8,256]{3,2,1,0:T(8,128)(2,1)S(1)}, u32[]{:S(2)}, u32[]{:S(2)}) async-start(bf16[256,2,8,256]{3,2,1,0:T(8,128)(2,1)} %copy.19), calls=%async_computation | async-start | bytes 4194304 | tf_op jit(solution)/shard_map/all_to_all | solution.py:62
Sparse Core Ops, SparseCore 0:
  506.5 29.4 all-gather.1
where the time goes:
time: 583 us; the launch traced here: 581 us
  local copies, waits for them, and re-layouts  491 us (84%)
  waiting for transfers between devices  55.1 us (9%)
  between operations  13.5 us (2%)
  starting transfers between devices  8.48 us (1%)
  matrix products  7.77 us (1%)
    gather x2, local copies, waits for them, and re-layouts, toeplitz(): picked = jnp.take(fir_taps, jnp.clip(lag_idx, 0, tap_count - 1), axis=1)  485 us
    all_gather x1, waiting for transfers between devices, shards(): gathered = lax.all_gather(spectra, 'chan', axis=3, tiled=True)  29.6 us
    all_to_all x1, waiting for transfers between devices, shards(): lax.all_to_all(gathered, 'tm', split_axis=0, concat_axis=2, tiled=True)  25.5 us
  transfers between devices with their start and end apart: 3, of which 2 were waited for; matrix products, arithmetic and copies ran while one was open for 84% of the time, Pallas kernels for 0%

commit v1 on v0

--- a/solution.py
+++ b/solution.py
@@ -59,7 +59,9 @@
         "csn,npk->kpsc", segments, make_table(), preferred_element_type=jnp.float32
     ).astype(jnp.bfloat16)
     gathered = lax.all_gather(spectra, "chan", axis=3, tiled=True)
-    all_bins = lax.all_to_all(gathered, "tm", split_axis=0, concat_axis=2, tiled=True)
+    pieces = jnp.split(gathered, lax.axis_size("tm"), axis=0)
+    incoming = lax.all_to_all(jnp.stack(pieces), "tm", 0, 0)
+    all_bins = jnp.concatenate(incoming, axis=2)
     factor = 1.0 / (all_bins.shape[2] * SEG)
     first_col = lax.axis_index("chan") * channels
     own_bins = lax.dynamic_slice_in_dim(all_bins, first_col, channels, 3)

time: 583 us -> 590 us (1.012)
    another operation x0 -> x2, local copies, waits for them, and re-layouts: none -> 8.67 us  [shards(): incoming = lax.all_to_all(jnp.stack(pieces), 'tm', 0, 0)]
  transfers between devices with their start and end apart: 3 -> 3, of which waited for: 2 -> 2; matrix products, arithmetic and copies ran while one was open for 84% -> 83% of each run, Pallas kernels for 0% -> 0%
where the time goes in v1:
time: 590 us; the launch traced here: 589 us
  local copies, waits for them, and re-layouts  496 us (84%)
  waiting for transfers between devices  55.1 us (9%)
  between operations  13.5 us (2%)
  starting transfers between devices  8.48 us (1%)
  other arithmetic  8.19 us (1%)
  matrix products  7.77 us (1%)
    gather x2, local copies, waits for them, and re-layouts, toeplitz(): picked = jnp.take(fir_taps, jnp.clip(lag_idx, 0, tap_count - 1), axis=1)  485 us
    all_gather x1, waiting for transfers between devices, shards(): gathered = lax.all_gather(spectra, 'chan', axis=3, tiled=True)  29.6 us
    all_to_all x1, waiting for transfers between devices, shards(): incoming = lax.all_to_all(jnp.stack(pieces), 'tm', 0, 0)  25.5 us
  transfers between devices with their start and end apart: 3, of which 2 were waited for; matrix products, arithmetic and copies ran while one was open for 83% of the time, Pallas kernels for 0%

profile of v1, /device:TPU:0, one launch (start us, length us, event | category | flops | bytes accessed | tf_op | source)
XLA Modules:
  0.0 588.9 jit_solution(16498076237917534550)
XLA Ops:
  6.5 0.0 all-gather.2.cloned.1.call-start
  6.5 0.7 slice.15
  7.3 4.8 collective-permute-start
  12.2 0.1 fusion.24
  12.4 0.3 copy.23
  12.6 0.1 broadcast_clamp_fusion
  12.7 2.3 multiply_convert_fusion
  15.0 0.4 fusion.37
  15.4 0.8 copy.13
  16.2 454.0 %gather_fusion = bf16[131072,32]{1,0:T(8,128)(2,1)} fusion(bf16[32,256]{0,1:T(8,128)(2,1)S(1)} %copy.13, s32[131072]{0:T(1024)S(1)} %broadcast_clamp_fusion), kind=kCustom, calls=%fused_computation | custom fusion | bytes 17301504 | tf_op jit(solution)/shard_map/jit(_take)/gather | solution.py:33
  470.2 0.0 copy-start
  470.2 30.7 %copy.14 = bf16[512,256,32]{1,0,2:T(8,128)(2,1)} copy(bf16[512,256,32]{2,1,0:T(8,128)(2,1)} %bitcast.42) | data formatting | bytes 16777216 | tf_op jit(solution)/shard_map/jit(_take)/gather | solution.py:33
  500.9 0.0 collective-permute-done
  500.9 0.0 copy-done
  501.0 0.1 reshape.218
  501.1 0.1 fusion.49
  501.2 4.7 fusion.15
  506.0 0.1 convert_element_type.45
  506.1 1.0 fusion.18
  507.1 0.0 all-gather.2.cloned.1.call-update
  507.1 29.6 %all-gather.2.cloned.1.call-done = bf16[256,2,8,256]{0,3,2,1:T(8,128)(2,1)} async-done(((bf16[256,2,8,32]{0,3,2,1:T(8,128)(2,1)}), bf16[256,2,8,256]{0,3,2,1:T(8,128)(2,1)}) %all-gather.2.cloned.1.call-update) | async-done | bytes 2097168 | tf_op jit(solution)/shard_map/all_gather | solution.py:61
  536.7 3.0 slice_bitcast_fusion.3
  539.7 2.6 pad_maximum_fusion
  542.3 5.6 copy.16
  547.9 3.6 all-to-all-start
  551.6 25.5 %all-to-all-done = bf16[4,64,2,8,256]{4,3,2,1,0:T(8,128)(2,1)S(1)} async-done(((bf16[4,64,2,8,256]{4,3,2,1,0:T(8,128)(2,1)}), bf16[4,64,2,8,256]{4,3,2,1,0:T(8,128)(2,1)S(1)}, u32[]{:S(2)}, u32[]{:S(2)}) %all-to-all-start) | async-done | bytes 2097184 | tf_op jit(solution)/shard_map/all_to_all | solution.py:63
  577.1 0.3 copy.29
  577.4 0.1 slice_negate_fusion
  577.5 1.0 convolution_bitcast_fusion
  578.5 1.0 fusion.12
  579.6 2.5 maximum_multiply_fusion
  (4 shorter events, 0.1 us)
Async XLA Ops:
  6.5 530.1 %all-gather.2.cloned.1.call-start = ((), (), s32[]{:S(2)}) async-start(), calls=%async_computation.1 | async-start | bytes 2359296 | tf_op jit(solution)/shard_map/all_gather | solution.py:61
  7.3 493.7 %collective-permute-start = (bf16[32,256]{1,0:T(8,128)(2,1)S(1)}, bf16[32,256]{1,0:T(8,128)(2,1)S(1)}, u32[]{:S(2)}, u32[]{:S(2)}) collective-permute-start(bf16[32,256]{1,0:T(8,128)(2,1)S(1)} %slice.15), channel_id=1, source_target_pairs={{0,8},{8,16},{16,24},{1,9},{9,17},{17,25},{2,10},{10,18},{18,26},{... | collective-permute-start | bytes 49160 | tf_op jit(solution)/shard_map/ppermute | solution.py:13
  470.2 30.7 %copy-start = (bf16[32,4096]{1,0:T(8,128)(2,1)S(1)}, bf16[32,4096]{1,0:T(8,128)(2,1)}, u32[]{:S(2)}) copy-start(bf16[32,4096]{1,0:T(8,128)(2,1)} %param.2) | copy-start | bytes 786436
  547.9 29.1 %all-to-all-start = ((bf16[4,64,2,8,256]{4,3,2,1,0:T(8,128)(2,1)}), bf16[4,64,2,8,256]{4,3,2,1,0:T(8,128)(2,1)S(1)}, u32[]{:S(2)}, u32[]{:S(2)}) async-start(bf16[4,64,2,8,256]{4,3,2,1,0:T(8,128)(2,1)} %copy.16), calls=%async_computation | async-start | bytes 4194304 | tf_op jit(solution)/shard_map/all_to_all | solution.py:63
Sparse Core Ops, SparseCore 0:
  507.2 29.4 all-gather.1
